TPU v7x, 32 devices: a whole 2x2x4 slice. The times are simulated.
32 devices in a mesh: grp: 2 (over x), tm: 16 (over z, y, core).
Axes of the slice: x: 2, y: 2, z: 4, core: 2. Of those that a mesh axis runs over, the one named last changes fastest.
Arguments:
- signals: bfloat16 [8, 1024, 256], P('grp', 'tm'), parts along dimension 0, may hold values from -6 to 6
- targets: bfloat16 [8, 1024, 768], P('grp', 'tm'), parts along dimension 0, may hold values from -6 to 6
- decay_rate: float32 [4096], P('grp'), parts along dimension 0, may hold values from 0 to 0.125, as said below
- pole_angle: float32 [4096], P('grp'), parts along dimension 0, may hold values from -3.1416 to 3.1416
- in_map: bfloat16 [8192, 256], P('grp'), parts along dimension 0
- out_map: bfloat16 [8192, 768], P('grp'), parts along dimension 0
Outputs:
- out_update: float32 [8192, 768], P(('grp', 'tm')), parts along dimension 0
- in_update: float32 [8192, 256], P(('grp', 'tm')), parts along dimension 0
- boundary_adjoint: float32 [8, 16, 4096], P('grp', 'tm'), parts along dimension 0
There are 2 independent parts, one for each index of `grp`. A program takes and returns all parts, laid end to end along the dimension named above; each array names one. Nothing has to cross between parts.
Inputs may be any that keep to these rules, and one draw needn't show every extreme that they name: Every mode decays: exp(-decay_rate) lies below 1.
All inputs are finite; a program needn't handle non-finite values.
Results may differ from a plain program's by a relative error of at most 0.0027.
Values sent between devices are 32-bit elements; how exact they have to be, the bound alone decides.
No kernel may reach another device: no remote copies, remote signals or barrier semaphores. Data moves between devices by JAX's collectives and lax.ppermute only.
A program may use at most 128 MiB of HBM per device.

v0:
```python
import math

import jax
import jax.numpy as jnp
from jax import lax
from jax.sharding import PartitionSpec as P


def cmul(first, second):
    half = first.shape[-1] // 2
    fr = first[..., :half]
    fi = first[..., half:]
    sr = second[..., :half]
    si = second[..., half:]
    return jnp.concatenate([fr * sr - fi * si, fr * si + fi * sr], axis=-1)


def mode_powers(decay_rate, angle, unit, counts):
    phase = jnp.mod(angle * unit, 2.0 * math.pi) * counts
    magnitude = jnp.exp(-decay_rate * unit * counts)
    return jnp.concatenate([magnitude * jnp.cos(phase), magnitude * jnp.sin(phase)], axis=-1)


def per_device(signals, targets, decay_rate, pole_angle, in_map, out_map):
    group = signals.shape[1]
    modes = decay_rate.shape[0]
    width = 2 * modes
    position = lax.axis_index("tm")
    rate_row = decay_rate[None, :]
    fwd_angle = pole_angle[None, :]
    rev_angle = -pole_angle[None, :]
    gain = jnp.sqrt(-jnp.expm1(-2.0 * decay_rate))
    gain_pair = jnp.concatenate([gain, gain])
    unit_one = jnp.ones((1, 1), jnp.float32)
    drive = (
        lax.dot_general(
            signals, in_map, (((2,), (1,)), ((), ())), preferred_element_type=jnp.float32
        )
        * gain_pair
    )
    local = drive
    span = 1
    while span < group:
        factor = mode_powers(rate_row, fwd_angle, float(span), unit_one)
        local = jnp.concatenate(
            [local[:, :span], local[:, span:] + cmul(factor[None], local[:, :-span])], axis=1
        )
        span = span * 2
    ends = local[:, group - 1]
    piece = lax.all_gather(ends[None], "tm", axis=0, tiled=True)
    index = jnp.arange(piece.shape[0], dtype=jnp.int32)
    gap = position - 1 - index
    used = (gap >= 0).astype(jnp.float32)[:, None]
    counts = jnp.maximum(gap, 0).astype(jnp.float32)[:, None]
    weights = mode_powers(rate_row, fwd_angle, float(group), counts) * used
    entering = jnp.sum(cmul(weights[:, None, :], piece), axis=0)
    offsets = (jnp.arange(group, dtype=jnp.float32) + 1.0)[:, None]
    fwd_table = mode_powers(rate_row, fwd_angle, 1.0, offsets)
    states = local + cmul(fwd_table[None], entering[:, None, :])
    states_b = states.astype(jnp.bfloat16)
    predicted = lax.dot_general(
        states_b, out_map, (((2,), (0,)), ((), ())), preferred_element_type=jnp.float32
    )
    misfit_b = (predicted - targets.astype(jnp.float32)).astype(jnp.bfloat16)
    back = lax.dot_general(
        misfit_b, out_map, (((2,), (1,)), ((), ())), preferred_element_type=jnp.float32
    )
    retro = back
    span = 1
    while span < group:
        factor = mode_powers(rate_row, rev_angle, float(span), unit_one)
        retro = jnp.concatenate(
            [retro[:, :-span] + cmul(factor[None], retro[:, span:]), retro[:, group - span :]],
            axis=1,
        )
        span = span * 2
    starts = retro[:, 0]
    piece = lax.all_gather(starts[None], "tm", axis=0, tiled=True)
    index = jnp.arange(piece.shape[0], dtype=jnp.int32)
    gap = index - position - 1
    used = (gap >= 0).astype(jnp.float32)[:, None]
    counts = jnp.maximum(gap, 0).astype(jnp.float32)[:, None]
    weights = mode_powers(rate_row, rev_angle, float(group), counts) * used
    later = jnp.sum(cmul(weights[:, None, :], piece), axis=0)
    remaining = (float(group) - jnp.arange(group, dtype=jnp.float32))[:, None]
    rev_table = mode_powers(rate_row, rev_angle, 1.0, remaining)
    adjoint = retro + cmul(rev_table[None], later[:, None, :])
    scaled = adjoint * gain_pair
    adjoint_b = scaled.astype(jnp.bfloat16)
    boundary_adjoint = scaled[:, 0:1, :]
    joined = lax.psum_scatter(
        jnp.concatenate(
            [
                lax.dot_general(
                    states_b,
                    misfit_b,
                    (((0, 1), (0, 1)), ((), ())),
                    preferred_element_type=jnp.float32,
                ),
                lax.dot_general(
                    adjoint_b,
                    signals,
                    (((0, 1), (0, 1)), ((), ())),
                    preferred_element_type=jnp.float32,
                ),
            ],
            axis=1,
        ),
        "tm",
        scatter_dimension=0,
        tiled=True,
    )
    out_grad = joined[:, : out_map.shape[1]]
    in_grad = joined[:, out_map.shape[1] :]
    out_square, in_square = lax.psum(
        (jnp.sum(out_grad * out_grad), jnp.sum(in_grad * in_grad)), "tm"
    )
    out_update = out_grad * lax.rsqrt(out_square / float(width * out_map.shape[1]) + 1e-06)
    in_update = in_grad * lax.rsqrt(in_square / float(width * in_map.shape[1]) + 1e-06)
    return (out_update, in_update, boundary_adjoint)


def solution(mesh):
    return jax.shard_map(
        per_device,
        mesh=mesh,
        in_specs=(
            P("grp", "tm", None),
            P("grp", "tm", None),
            P("grp"),
            P("grp"),
            P("grp", None),
            P("grp", None),
        ),
        out_specs=(P(("grp", "tm"), None), P(("grp", "tm"), None), P("grp", "tm", None)),
        check_vma=False,
    )
```

profile of v0, /device:TPU:0, one launch (start us, length us, event | category | flops | bytes accessed | tf_op | source)
XLA Modules:
  0.0 376.9 jit_solution(7007309276360066433)
XLA Ops:
  7.2 1.3 cosine_multiply_fusion
  8.8 1.6 convolution_multiply_fusion
  20.4 1.7 fusion.15
  28.8 3.9 %fusion.29 = (f32[64,2048]{1,0:T(8,128)S(1)}, f32[64,2048]{1,0:T(8,128)S(1)}, f32[64,2048]{1,0:T(8,128)S(1)}, f32[64,2048]{1,0:T(8,128)S(1)}) fusion(f32[2048]{0:T(1024)S(1)} %get-tuple-element.116, f32[64]{0:T(128)S(1)} %iota_subtract_fusion, f32[2048]{0:T(1024)S(1)} %get-tuple-element.118, f32[2048]{0:T(1024)S(1)} %get-tuple-element.123, ...), kind=kLoop, calls=%fused_computation.110 | loop fusion | flops 1048576 | bytes 2122240 | tf_op jit(solution)/shard_map/mul | solution.py:21
  32.6 1.1 maximum_bitcast_fusion
  33.8 1.1 slice_bitcast_fusion.3
  34.8 28.8 %all-gather.5.cloned.1.call-done = f32[64,1,4096]{2,1,0:T(1,128)} async-done(((f32[4,1,4096]{2,1,0:T(1,128)}), f32[64,1,4096]{2,1,0:T(1,128)}) %all-gather.5.cloned.1.call-update) | async-done | bytes 1048592 | tf_op jit(solution)/shard_map/all_gather | solution.py:50
  63.6 3.7 reduce
  67.3 1.3 reshape.510
  68.6 1.6 multiply_subtract_fusion.15
  72.9 1.3 copy-done.5
  74.3 1.8 fusion.23
  76.1 2.1 fusion
  88.0 1.3 copy-done.7
  90.4 1.9 slice_bitcast_fusion.5
  92.2 2.3 slice_bitcast_fusion.1
  94.5 6.4 %convolution_bitcast_fusion = f32[4096,768]{0,1:T(8,128)} fusion(bf16[4,64,4096]{2,1,0:T(8,128)(2,1)S(1)} %copy-done.6, bf16[4,64,768]{2,1,0:T(8,128)(2,1)S(1)} %fusion.23), kind=kOutput, calls=%fused_computation.7 | convolution fusion | flops 1610612736 | bytes 15073280 | tf_op jit(solution)/shard_map/dot_general | solution.py:94
  100.9 26.1 %all-gather.7.cloned.1.call-done = f32[64,1,4096]{2,1,0:T(1,128)} async-done(((f32[4,1,4096]{2,1,0:T(1,128)}), f32[64,1,4096]{2,1,0:T(1,128)}) %all-gather.7.cloned.1.call-update) | async-done | bytes 1048592 | tf_op jit(solution)/shard_map/all_gather | solution.py:78
  127.0 4.8 %reduce.1 = f32[64,4096]{1,0:T(8,128)} reduce(f32[64,1,4096]{2,1,0:T(1,128)} %all-gather.7.cloned.1.call-done, f32[]{:T(128)} %constant.75), dimensions={1}, to_apply=%all-gather.1.reduce_sub_computation | reduce | bytes 2097156 | tf_op jit(solution)/shard_map/all_gather | solution.py:78
  131.8 2.5 reshape.511
  134.3 1.6 multiply_subtract_fusion.14
  138.7 2.1 copy-done.2
  141.8 1.3 slice-done.1
  143.1 1.4 slice-done.2
  144.5 6.1 %pad_maximum_fusion = f32[4096,1024]{0,1:T(8,128)} fusion(f32[4096,256]{0,1:T(8,128)S(1)} %convolution_bitcast_fusion.1, f32[4096,768]{0,1:T(8,128)S(1)} %bitcast.133), kind=kLoop, calls=%fused_computation | loop fusion | flops 4194304 | bytes 33554432 | tf_op jit(solution)/shard_map/concatenate | solution.py:92
  150.6 176.2 %reduce-scatter.2.cloned.1.call-done = f32[256,1024]{0,1:T(8,128)} async-done(((f32[4096,1024]{0,1:T(8,128)}), f32[256,1024]{0,1:T(8,128)}) %reduce-scatter.2.cloned.1.call-update) | async-done | bytes 1048592 | tf_op jit(solution)/shard_map/reduce_scatter | solution.py:91
  326.8 1.6 multiply_reduce_fusion.1
  328.5 1.9 multiply_reduce_fusion
  330.4 1.7 slice.496
  332.1 32.1 %all-reduce = (f32[]{:T(128)}, f32[]{:T(128)}) all-reduce(f32[]{:T(128)} %multiply_reduce_fusion, f32[]{:T(128)} %multiply_reduce_fusion.1), channel_id=1, replica_groups=mesh['grp'=2,'tm'=16] {'tm'}, use_global_device_ids=true, to_apply=%region_4.5 | all-reduce | flops 2 | bytes 16 | tf_op jit(solution)/shard_map/psum | solution.py:115
  365.6 1.3 slice_multiply_fusion
  367.0 1.1 copy.11
  (155 shorter events, 35.5 us)
Async XLA Ops:
  7.2 1.6 copy-start
  7.2 56.4 %all-gather.5.cloned.1.call-start = ((), (), s32[]{:S(2)}) async-start(), calls=%async_computation.2 | async-start | bytes 1114112 | tf_op jit(solution)/shard_map/all_gather | solution.py:50
  22.8 104.2 %all-gather.7.cloned.1.call-start = ((), (), s32[]{:S(2)}) async-start(), calls=%async_computation.3 | async-start | bytes 1114112 | tf_op jit(solution)/shard_map/all_gather | solution.py:78
  68.6 1.8 copy-start.12
  68.6 1.8 copy-start.13
  70.5 1.6 copy-start.9
  70.5 3.8 %slice-start.3 = ((s8[6291456]{0:T(1024)(128)(4,1)}), s8[4194304]{0:T(1024)(128)(4,1)S(1)}, s32[]{:S(2)}) async-start(s8[6291456]{0:T(1024)(128)(4,1)} %bitcast.134), calls=%async_computation.7 | async-start | bytes 8388608
  72.1 2.2 slice-start.4
  72.1 2.3 copy-start.29
  72.9 1.3 copy-start.5
  76.1 2.2 copy-start.23
  76.1 2.2 copy-start.24
  79.2 0.7 copy-start.28
  81.7 0.7 copy-start.26
  83.1 0.7 copy-start.22
  85.4 1.5 copy-start.3
  86.5 0.7 copy-start.18
  88.0 1.3 copy-start.7
  90.0 236.8 %reduce-scatter.2.cloned.1.call-start = ((), (), s32[]{:S(2)}) async-start(), calls=%async_computation.1 | async-start | bytes 17825792 | tf_op jit(solution)/shard_map/reduce_scatter | solution.py:91
  90.3 4.1 %copy-start.6 = (bf16[4,64,4096]{2,1,0:T(8,128)(2,1)S(1)}, bf16[4,64,4096]{2,1,0:T(8,128)(2,1)}, u32[]{:S(2)}) copy-start(bf16[4,64,4096]{2,1,0:T(8,128)(2,1)} %copy-done.5) | copy-start | bytes 6291460
  100.9 33.4 %copy-start.15 = (f32[16,2048]{1,0:T(8,128)S(1)}, f32[16,2048]{1,0:T(8,128)}, u32[]{:S(2)}) copy-start(f32[16,2048]{1,0:T(8,128)} %get-tuple-element.50) | copy-start | bytes 393220
  100.9 33.4 %copy-start.16 = (f32[16,2048]{1,0:T(8,128)S(1)}, f32[16,2048]{1,0:T(8,128)}, u32[]{:S(2)}) copy-start(f32[16,2048]{1,0:T(8,128)} %get-tuple-element.51) | copy-start | bytes 393220
  134.3 1.8 copy-start.10
  134.3 1.8 copy-start.11
  136.1 1.2 copy-start.4
  136.1 1.9 copy-start.8
  138.0 2.8 copy-start.14
  138.0 3.8 %slice-start = ((s8[12582912]{0:T(1024)(128)(4,1)}), s8[4194304]{0:T(1024)(128)(4,1)S(1)}, s32[]{:S(2)}) async-start(s8[12582912]{0:T(1024)(128)(4,1)} %bitcast.132), calls=%async_computation.4 | async-start | bytes 8388608
  138.0 5.0 %slice-start.1 = ((s8[12582912]{0:T(1024)(128)(4,1)}), s8[4194304]{0:T(1024)(128)(4,1)S(1)}, s32[]{:S(2)}) async-start(s8[12582912]{0:T(1024)(128)(4,1)} %bitcast.132), calls=%async_computation.5 | async-start | bytes 8388608
  138.7 2.1 copy-start.2
  140.8 3.7 slice-start.2
  365.6 4.3 %copy-start.1 = (bf16[4096,256]{1,0:T(8,128)(2,1)S(1)}, bf16[4096,256]{1,0:T(8,128)(2,1)}, u32[]{:S(2)}) copy-start(bf16[4096,256]{1,0:T(8,128)(2,1)} %param.10) | copy-start | bytes 6291460
  (6 other events, 4.2 us)
Sparse Core Ops, SparseCore 0:
  23.0 40.5 all-gather.4
  90.2 36.7 all-gather.6
  150.7 176.0 reduce-scatter.1
where the time goes:
time: 384 us; the launch traced here: 377 us
  waiting for transfers between devices  231 us (60%)
  other arithmetic  54.7 us (14%)
  blocking collectives  32.1 us (8%)
  local copies, waits for them, and re-layouts  29.3 us (8%)
  between operations  16.4 us (4%)
  matrix products  12.7 us (3%)
    reduce_scatter x1, waiting for transfers between devices, per_device(): lax.psum_scatter(jnp.concatenate([lax.dot_general(states_b, misfit_b, (((...  176 us
    psum x1, blocking collectives, per_device(): lax.psum((jnp.sum(out_grad * out_grad), jnp.sum(in_grad * in_grad)), 'tm')  32.1 us
    all_gather x1, waiting for transfers between devices, per_device(): piece = lax.all_gather(ends[None], 'tm', axis=0, tiled=True)  28.8 us
    all_gather x1, waiting for transfers between devices, per_device(): piece = lax.all_gather(starts[None], 'tm', axis=0, tiled=True)  26.1 us
    unnamed x72, local copies, waits for them, and re-layouts  13.2 us
    sub x16, other arithmetic, cmul(): return jnp.concatenate([fr * sr - fi * si, fr * si + fi * sr], axis=-1)  12.4 us
  transfers between devices with their start and end apart: 3, of which 3 were waited for; matrix products, arithmetic and copies ran while one was open for 6% of the time, Pallas kernels for 0%

commit v1 on v0

--- a/solution.py
+++ b/solution.py
@@ -21,11 +21,40 @@
     return jnp.concatenate([magnitude * jnp.cos(phase), magnitude * jnp.sin(phase)], axis=-1)
 
 
+def carry_in(values, rate_row, angle_row, group, count, reverse):
+    unit_one = jnp.ones((1, 1), jnp.float32)
+
+    def pairs(span):
+        if reverse:
+            return [(i + span, i) for i in range(count - span)]
+        return [(i, i + span) for i in range(count - span)]
+
+    if count == 1:
+        return jnp.zeros_like(values)
+    acc = lax.ppermute(values, "tm", pairs(1))
+    span = 1
+    while span < count:
+        factor = mode_powers(rate_row, angle_row, float(group * span), unit_one)
+        acc = acc + cmul(factor, lax.ppermute(acc, "tm", pairs(span)))
+        span = span * 2
+    return acc
+
+
+def tm_sum(value, count):
+    if count & (count - 1):
+        return lax.psum(value, "tm")
+    span = 1
+    while span < count:
+        value = value + lax.ppermute(value, "tm", [(i, i ^ span) for i in range(count)])
+        span = span * 2
+    return value
+
+
 def per_device(signals, targets, decay_rate, pole_angle, in_map, out_map):
     group = signals.shape[1]
     modes = decay_rate.shape[0]
     width = 2 * modes
-    position = lax.axis_index("tm")
+    count = lax.axis_size("tm")
     rate_row = decay_rate[None, :]
     fwd_angle = pole_angle[None, :]
     rev_angle = -pole_angle[None, :]
@@ -47,13 +76,7 @@
         )
         span = span * 2
     ends = local[:, group - 1]
-    piece = lax.all_gather(ends[None], "tm", axis=0, tiled=True)
-    index = jnp.arange(piece.shape[0], dtype=jnp.int32)
-    gap = position - 1 - index
-    used = (gap >= 0).astype(jnp.float32)[:, None]
-    counts = jnp.maximum(gap, 0).astype(jnp.float32)[:, None]
-    weights = mode_powers(rate_row, fwd_angle, float(group), counts) * used
-    entering = jnp.sum(cmul(weights[:, None, :], piece), axis=0)
+    entering = carry_in(ends, rate_row, fwd_angle, group, count, False)
     offsets = (jnp.arange(group, dtype=jnp.float32) + 1.0)[:, None]
     fwd_table = mode_powers(rate_row, fwd_angle, 1.0, offsets)
     states = local + cmul(fwd_table[None], entering[:, None, :])
@@ -75,47 +98,32 @@
         )
         span = span * 2
     starts = retro[:, 0]
-    piece = lax.all_gather(starts[None], "tm", axis=0, tiled=True)
-    index = jnp.arange(piece.shape[0], dtype=jnp.int32)
-    gap = index - position - 1
-    used = (gap >= 0).astype(jnp.float32)[:, None]
-    counts = jnp.maximum(gap, 0).astype(jnp.float32)[:, None]
-    weights = mode_powers(rate_row, rev_angle, float(group), counts) * used
-    later = jnp.sum(cmul(weights[:, None, :], piece), axis=0)
+    later = carry_in(starts, rate_row, rev_angle, group, count, True)
     remaining = (float(group) - jnp.arange(group, dtype=jnp.float32))[:, None]
     rev_table = mode_powers(rate_row, rev_angle, 1.0, remaining)
     adjoint = retro + cmul(rev_table[None], later[:, None, :])
     scaled = adjoint * gain_pair
     adjoint_b = scaled.astype(jnp.bfloat16)
     boundary_adjoint = scaled[:, 0:1, :]
-    joined = lax.psum_scatter(
-        jnp.concatenate(
-            [
-                lax.dot_general(
-                    states_b,
-                    misfit_b,
-                    (((0, 1), (0, 1)), ((), ())),
-                    preferred_element_type=jnp.float32,
-                ),
-                lax.dot_general(
-                    adjoint_b,
-                    signals,
-                    (((0, 1), (0, 1)), ((), ())),
-                    preferred_element_type=jnp.float32,
-                ),
-            ],
-            axis=1,
+    out_grad = lax.psum_scatter(
+        lax.dot_general(
+            states_b, misfit_b, (((0, 1), (0, 1)), ((), ())), preferred_element_type=jnp.float32
         ),
         "tm",
         scatter_dimension=0,
         tiled=True,
     )
-    out_grad = joined[:, : out_map.shape[1]]
-    in_grad = joined[:, out_map.shape[1] :]
-    out_square, in_square = lax.psum(
-        (jnp.sum(out_grad * out_grad), jnp.sum(in_grad * in_grad)), "tm"
+    in_grad = lax.psum_scatter(
+        lax.dot_general(
+            adjoint_b, signals, (((0, 1), (0, 1)), ((), ())), preferred_element_type=jnp.float32
+        ),
+        "tm",
+        scatter_dimension=0,
+        tiled=True,
     )
+    out_square = tm_sum(jnp.sum(out_grad * out_grad), count)
     out_update = out_grad * lax.rsqrt(out_square / float(width * out_map.shape[1]) + 1e-06)
+    in_square = tm_sum(jnp.sum(in_grad * in_grad), count)
     in_update = in_grad * lax.rsqrt(in_square / float(width * in_map.shape[1]) + 1e-06)
     return (out_update, in_update, boundary_adjoint)
 

time: 384 us -> 346 us (0.901); the launches traced: 377 us -> 345 us
  starting transfers between devices: 0.55 us -> 44.8 us
  blocking collectives: 32.1 us -> 0 us
  local copies, waits for them, and re-layouts: 29.3 us -> 7.91 us
  other arithmetic: 54.7 us -> 34.1 us
  waiting for transfers between devices: 231 us -> 223 us
  between operations: 16.4 us -> 21.1 us
    all_gather x2 -> x0, waiting for transfers between devices: 54.9 us -> none  [the longest x1 28.8 us: per_device(): piece = lax.all_gather(ends[None], 'tm', axis=0, tiled=True)]
    ppermute x0 -> x18, starting transfers between devices: none -> 44.7 us  [the longest x8 26 us: carry_in(): acc = acc + cmul(factor, lax.ppermute(acc, 'tm', pairs(span)))]
    ppermute x0 -> x18, waiting for transfers between devices: none -> 42.2 us  [the longest x8 28.1 us: carry_in(): acc = acc + cmul(factor, lax.ppermute(acc, 'tm', pairs(span)))]
    psum x1 -> x0, blocking collectives: 32.1 us -> none  [per_device(): lax.psum((jnp.sum(out_grad * out_grad), jnp.sum(in_grad * in_grad)), 'tm')]
    all_gather x2 -> x0, other arithmetic: 8.48 us -> none  [the longest x1 4.75 us: per_device(): piece = lax.all_gather(starts[None], 'tm', axis=0, tiled=True)]
    unnamed x72 -> x20, local copies, waits for them, and re-layouts: 13.2 us -> 5.39 us
    concatenate x2 -> x0, other arithmetic: 7.09 us -> none  [the longest x1 6.06 us: per_device(): jnp.concatenate([lax.dot_general(states_b, misfit_b, (((0, 1), (0, 1)), (...]
    mul x6 -> x4, local copies, waits for them, and re-layouts: 5.21 us -> 0.16 us  [cmul(): return jnp.concatenate([fr * sr - fi * si, fr * si + fi * sr], axis=-1)]
  transfers between devices with their start and end apart: 3 -> 20, of which waited for: 3 -> 19; matrix products, arithmetic and copies ran while one was open for 6% -> 5% of each run, Pallas kernels for 0% -> 0%
where the time goes in v1:
time: 346 us; the launch traced here: 345 us
  waiting for transfers between devices  223 us (64%)
  starting transfers between devices  44.8 us (13%)
  other arithmetic  34.1 us (10%)
  between operations  21.1 us (6%)
  matrix products  14.6 us (4%)
  local copies, waits for them, and re-layouts  7.91 us (2%)
    reduce_scatter x1, waiting for transfers between devices, per_device(): lax.psum_scatter(lax.dot_general(states_b, misfit_b, (((0, 1), (0, 1)), (...  118 us
    reduce_scatter x1, waiting for transfers between devices, per_device(): lax.psum_scatter(lax.dot_general(adjoint_b, signals, (((0, 1), (0, 1)), (...  62.3 us
    ppermute x8, waiting for transfers between devices, carry_in(): acc = acc + cmul(factor, lax.ppermute(acc, 'tm', pairs(span)))  28.1 us
    ppermute x8, starting transfers between devices, carry_in(): acc = acc + cmul(factor, lax.ppermute(acc, 'tm', pairs(span)))  26 us
    ppermute x8, starting transfers between devices, tm_sum(): lax.ppermute(value, 'tm', [(i, i ^ span) for i in range(count)])  14.8 us
    ppermute x8, waiting for transfers between devices, tm_sum(): lax.ppermute(value, 'tm', [(i, i ^ span) for i in range(count)])  12.2 us
    sub x22, other arithmetic, cmul(): return jnp.concatenate([fr * sr - fi * si, fr * si + fi * sr], axis=-1)  9.21 us
  transfers between devices with their start and end apart: 20, of which 19 were waited for; matrix products, arithmetic and copies ran while one was open for 5% of the time, Pallas kernels for 0%

profile of v1, /device:TPU:0, one launch (start us, length us, event | category | flops | bytes accessed | tf_op | source)
XLA Modules:
  0.0 345.3 jit_solution(8670590177126788704)
XLA Ops:
  21.2 2.6 collective-permute-start
  23.8 3.9 %fusion.29 = (f32[64,2048]{1,0:T(8,128)S(1)}, f32[64,2048]{1,0:T(8,128)S(1)}, f32[64,2048]{1,0:T(8,128)S(1)}, f32[64,2048]{1,0:T(8,128)S(1)}) fusion(f32[2048]{0:T(1024)S(1)} %get-tuple-element.128, f32[64]{0:T(128)S(1)} %iota_subtract_fusion, f32[2048]{0:T(1024)S(1)} %get-tuple-element.129, f32[2048]{0:T(1024)S(1)} %get-tuple-element.131, ...), kind=kLoop, calls=%fused_computation.106 | loop fusion | flops 1048576 | bytes 2122240 | tf_op jit(solution)/shard_map/mul | solution.py:21
  28.0 4.5 %collective-permute-start.1 = (f32[4,4096]{1,0:T(4,128)S(1)}, f32[4,4096]{1,0:T(4,128)S(1)}, u32[]{:S(2)}, u32[]{:S(2)}) collective-permute-start(f32[4,4096]{1,0:T(4,128)S(1)} %collective-permute-done), channel_id=1, source_target_pairs={{0,1},{1,2},{2,3},{3,4},{4,5},{5,6},{6,7},{7,8},{8,9},{9,10},{10,1... | collective-permute-start | bytes 196616 | tf_op jit(solution)/shard_map/ppermute | solution.py:38
  33.5 4.6 %collective-permute-start.2 = (f32[4,4096]{1,0:T(4,128)S(1)}, f32[4,4096]{1,0:T(4,128)S(1)}, u32[]{:S(2)}, u32[]{:S(2)}) collective-permute-start(f32[4,4096]{1,0:T(4,128)S(1)} %maximum_add_fusion.1), channel_id=1, source_target_pairs={{0,2},{1,3},{2,4},{3,5},{4,6},{5,7},{6,8},{7,9},{8,10},{9,11},{10,... | collective-permute-start | bytes 196616 | tf_op jit(solution)/shard_map/ppermute | solution.py:38
  38.1 1.9 collective-permute-done.2
  40.0 6.2 %collective-permute-start.3 = (f32[4,4096]{1,0:T(4,128)S(1)}, f32[4,4096]{1,0:T(4,128)S(1)}, u32[]{:S(2)}, u32[]{:S(2)}) collective-permute-start(f32[4,4096]{1,0:T(4,128)S(1)} %maximum_add_fusion.2), channel_id=1, source_target_pairs={{0,4},{1,5},{2,6},{3,7},{4,8},{5,9},{6,10},{7,11},{8,12},{9,13},{1... | collective-permute-start | bytes 196616 | tf_op jit(solution)/shard_map/ppermute | solution.py:38
  46.3 1.9 collective-permute-done.3
  48.2 5.3 %collective-permute-start.4 = (f32[4,4096]{1,0:T(4,128)S(1)}, f32[4,4096]{1,0:T(4,128)S(1)}, u32[]{:S(2)}, u32[]{:S(2)}) collective-permute-start(f32[4,4096]{1,0:T(4,128)S(1)} %maximum_add_fusion.3), channel_id=1, source_target_pairs={{0,8},{1,9},{2,10},{3,11},{4,12},{5,13},{6,14},{7,15},{16,24},{17,... | collective-permute-start | bytes 196616 | tf_op jit(solution)/shard_map/ppermute | solution.py:38
  53.5 1.9 collective-permute-done.4
  58.5 1.8 fusion.23
  60.3 1.8 fusion
  72.0 1.8 collective-permute-done.9
  75.1 2.0 collective-permute-done.10
  78.4 6.6 %collective-permute-done.11 = f32[4,4096]{1,0:T(4,128)S(1)} collective-permute-done((f32[4,4096]{1,0:T(4,128)S(1)}, f32[4,4096]{1,0:T(4,128)S(1)}, u32[]{:S(2)}, u32[]{:S(2)}) %collective-permute-start.11) | collective-permute-done | bytes 65568 | tf_op jit(solution)/shard_map/ppermute | solution.py:38
  86.4 7.7 %collective-permute-done.12 = f32[4,4096]{1,0:T(4,128)S(1)} collective-permute-done((f32[4,4096]{1,0:T(4,128)S(1)}, f32[4,4096]{1,0:T(4,128)S(1)}, u32[]{:S(2)}, u32[]{:S(2)}) %collective-permute-start.12) | collective-permute-done | bytes 65568 | tf_op jit(solution)/shard_map/ppermute | solution.py:38
  95.7 5.5 %collective-permute-done.13 = f32[4,4096]{1,0:T(4,128)S(1)} collective-permute-done((f32[4,4096]{1,0:T(4,128)S(1)}, f32[4,4096]{1,0:T(4,128)S(1)}, u32[]{:S(2)}, u32[]{:S(2)}) %collective-permute-start.13) | collective-permute-done | bytes 65568 | tf_op jit(solution)/shard_map/ppermute | solution.py:38
  102.5 2.0 copy-done.2
  104.5 2.7 convolution_bitcast_fusion.1
  108.8 6.6 %convolution_bitcast_fusion = f32[4096,768]{1,0:T(8,128)} fusion(bf16[4,64,4096]{2,1,0:T(8,128)(2,1)S(1)} %copy-done.4, bf16[4,64,768]{2,1,0:T(8,128)(2,1)S(1)} %fusion.23), kind=kOutput, calls=%fused_computation.6 | convolution fusion | flops 1610612736 | bytes 15073280 | tf_op jit(solution)/shard_map/dot_general | solution.py:109
  115.4 1.9 slice.526
  117.3 62.3 %reduce-scatter.5.cloned.1.call-done = f32[256,256]{1,0:T(8,128)} async-done(((f32[4096,256]{1,0:T(8,128)}), f32[256,256]{1,0:T(8,128)}) %reduce-scatter.5.cloned.1.call-update) | async-done | bytes 262160 | tf_op jit(solution)/shard_map/reduce_scatter | solution.py:116
  183.9 1.8 collective-permute-start.15
  185.8 1.9 collective-permute-done.15
  188.2 2.2 collective-permute-start.16
  192.6 2.7 collective-permute-start.17
  195.2 2.0 collective-permute-done.17
  199.5 118.2 %reduce-scatter.3.cloned.1.call-done = f32[256,768]{1,0:T(8,128)} async-done(((f32[4096,768]{1,0:T(8,128)}), f32[256,768]{1,0:T(8,128)}) %reduce-scatter.3.cloned.1.call-update) | async-done | bytes 786448 | tf_op jit(solution)/shard_map/reduce_scatter | solution.py:108
  317.7 1.9 multiply_reduce_fusion
  322.3 2.8 collective-permute-start.6
  326.7 2.3 collective-permute-start.7
  331.1 3.0 collective-permute-start.8
  336.4 2.1 broadcast_multiply_fusion
  (133 shorter events, 48.0 us)
Async XLA Ops:
  7.2 1.8 copy-start
  7.2 172.5 %reduce-scatter.5.cloned.1.call-start = ((), (), s32[]{:S(2)}) async-start(), calls=%async_computation.3 | async-start | bytes 4456448 | tf_op jit(solution)/shard_map/reduce_scatter | solution.py:116
  21.2 6.9 %collective-permute-start = (f32[4,4096]{1,0:T(4,128)S(1)}, f32[4,4096]{1,0:T(4,128)S(1)}, u32[]{:S(2)}, u32[]{:S(2)}) collective-permute-start(f32[4,4096]{1,0:T(4,128)S(1)} %bitcast.134), channel_id=1, source_target_pairs={{0,1},{1,2},{2,3},{3,4},{4,5},{5,6},{6,7},{7,8},{8,9},{9,10},{10,1... | collective-permute-start | bytes 196616 | tf_op jit(solution)/shard_map/ppermute | solution.py:34
  28.0 5.4 %collective-permute-start.1 = (f32[4,4096]{1,0:T(4,128)S(1)}, f32[4,4096]{1,0:T(4,128)S(1)}, u32[]{:S(2)}, u32[]{:S(2)}) collective-permute-start(f32[4,4096]{1,0:T(4,128)S(1)} %collective-permute-done), channel_id=1, source_target_pairs={{0,1},{1,2},{2,3},{3,4},{4,5},{5,6},{6,7},{7,8},{8,9},{9,10},{10,1... | collective-permute-start | bytes 196616 | tf_op jit(solution)/shard_map/ppermute | solution.py:38
  33.5 6.5 %collective-permute-start.2 = (f32[4,4096]{1,0:T(4,128)S(1)}, f32[4,4096]{1,0:T(4,128)S(1)}, u32[]{:S(2)}, u32[]{:S(2)}) collective-permute-start(f32[4,4096]{1,0:T(4,128)S(1)} %maximum_add_fusion.1), channel_id=1, source_target_pairs={{0,2},{1,3},{2,4},{3,5},{4,6},{5,7},{6,8},{7,9},{8,10},{9,11},{10,... | collective-permute-start | bytes 196616 | tf_op jit(solution)/shard_map/ppermute | solution.py:38
  40.0 8.1 %collective-permute-start.3 = (f32[4,4096]{1,0:T(4,128)S(1)}, f32[4,4096]{1,0:T(4,128)S(1)}, u32[]{:S(2)}, u32[]{:S(2)}) collective-permute-start(f32[4,4096]{1,0:T(4,128)S(1)} %maximum_add_fusion.2), channel_id=1, source_target_pairs={{0,4},{1,5},{2,6},{3,7},{4,8},{5,9},{6,10},{7,11},{8,12},{9,13},{1... | collective-permute-start | bytes 196616 | tf_op jit(solution)/shard_map/ppermute | solution.py:38
  48.2 7.2 %collective-permute-start.4 = (f32[4,4096]{1,0:T(4,128)S(1)}, f32[4,4096]{1,0:T(4,128)S(1)}, u32[]{:S(2)}, u32[]{:S(2)}) collective-permute-start(f32[4,4096]{1,0:T(4,128)S(1)} %maximum_add_fusion.3), channel_id=1, source_target_pairs={{0,8},{1,9},{2,10},{3,11},{4,12},{5,13},{6,14},{7,15},{16,24},{17,... | collective-permute-start | bytes 196616 | tf_op jit(solution)/shard_map/ppermute | solution.py:38
  55.4 2.2 slice-start
  56.0 2.4 slice-start.1
  56.0 2.4 copy-start.6
  58.5 1.8 copy-start.3
  70.7 3.1 collective-permute-start.9
  73.8 3.2 collective-permute-start.10
  77.1 7.9 %collective-permute-start.11 = (f32[4,4096]{1,0:T(4,128)S(1)}, f32[4,4096]{1,0:T(4,128)S(1)}, u32[]{:S(2)}, u32[]{:S(2)}) collective-permute-start(f32[4,4096]{1,0:T(4,128)S(1)} %maximum_add_fusion.5), channel_id=1, source_target_pairs={{2,0},{3,1},{4,2},{5,3},{6,4},{7,5},{8,6},{9,7},{10,8},{11,9},{12,... | collective-permute-start | bytes 196616 | tf_op jit(solution)/shard_map/ppermute | solution.py:38
  85.1 9.0 %collective-permute-start.12 = (f32[4,4096]{1,0:T(4,128)S(1)}, f32[4,4096]{1,0:T(4,128)S(1)}, u32[]{:S(2)}, u32[]{:S(2)}) collective-permute-start(f32[4,4096]{1,0:T(4,128)S(1)} %maximum_add_fusion.6), channel_id=1, source_target_pairs={{4,0},{5,1},{6,2},{7,3},{8,4},{9,5},{10,6},{11,7},{12,8},{13,9},{1... | collective-permute-start | bytes 196616 | tf_op jit(solution)/shard_map/ppermute | solution.py:38
  94.1 7.1 %collective-permute-start.13 = (f32[4,4096]{1,0:T(4,128)S(1)}, f32[4,4096]{1,0:T(4,128)S(1)}, u32[]{:S(2)}, u32[]{:S(2)}) collective-permute-start(f32[4,4096]{1,0:T(4,128)S(1)} %maximum_add_fusion.7), channel_id=1, source_target_pairs={{8,0},{9,1},{10,2},{11,3},{12,4},{13,5},{14,6},{15,7},{24,16},{25,... | collective-permute-start | bytes 196616 | tf_op jit(solution)/shard_map/ppermute | solution.py:38
  101.8 2.6 copy-start.5
  102.5 2.0 copy-start.2
  107.2 1.6 copy-start.4
  107.2 210.5 %reduce-scatter.3.cloned.1.call-start = ((), (), s32[]{:S(2)}) async-start(), calls=%async_computation.2 | async-start | bytes 13369344 | tf_op jit(solution)/shard_map/reduce_scatter | solution.py:108
  115.4 223.1 %copy-start.1 = (bf16[4096,256]{1,0:T(8,128)(2,1)S(1)}, bf16[4096,256]{1,0:T(8,128)(2,1)}, u32[]{:S(2)}) copy-start(bf16[4096,256]{1,0:T(8,128)(2,1)} %param.10) | copy-start | bytes 6291460
  181.3 1.4 collective-permute-start.14
  183.9 3.7 %collective-permute-start.15 = (f32[]{:T(128)}, f32[]{:T(128)}, u32[]{:S(2)}, u32[]{:S(2)}) collective-permute-start(f32[]{:T(128)} %add.355), channel_id=1, source_target_pairs={{0,2},{1,3},{2,0},{3,1},{4,6},{5,7},{6,4},{7,5},{8,10},{9,11},{10,... | collective-permute-start | bytes 20 | tf_op jit(solution)/shard_map/ppermute | solution.py:48
  188.2 3.7 %collective-permute-start.16 = (f32[]{:T(128)}, f32[]{:T(128)}, u32[]{:S(2)}, u32[]{:S(2)}) collective-permute-start(f32[]{:T(128)} %add.356), channel_id=1, source_target_pairs={{0,4},{1,5},{2,6},{3,7},{4,0},{5,1},{6,2},{7,3},{8,12},{9,13},{10,... | collective-permute-start | bytes 20 | tf_op jit(solution)/shard_map/ppermute | solution.py:48
  192.6 4.6 %collective-permute-start.17 = (f32[]{:T(128)}, f32[]{:T(128)}, u32[]{:S(2)}, u32[]{:S(2)}) collective-permute-start(f32[]{:T(128)} %add.357), channel_id=1, source_target_pairs={{0,8},{1,9},{2,10},{3,11},{4,12},{5,13},{6,14},{7,15},{8,0},{9,1},... | collective-permute-start | bytes 20 | tf_op jit(solution)/shard_map/ppermute | solution.py:48
  319.6 1.4 collective-permute-start.5
  322.3 3.7 %collective-permute-start.6 = (f32[]{:T(128)}, f32[]{:T(128)}, u32[]{:S(2)}, u32[]{:S(2)}) collective-permute-start(f32[]{:T(128)} %add.318), channel_id=1, source_target_pairs={{0,2},{1,3},{2,0},{3,1},{4,6},{5,7},{6,4},{7,5},{8,10},{9,11},{10,... | collective-permute-start | bytes 20 | tf_op jit(solution)/shard_map/ppermute | solution.py:48
  326.7 3.7 %collective-permute-start.7 = (f32[]{:T(128)}, f32[]{:T(128)}, u32[]{:S(2)}, u32[]{:S(2)}) collective-permute-start(f32[]{:T(128)} %add.319), channel_id=1, source_target_pairs={{0,4},{1,5},{2,6},{3,7},{4,0},{5,1},{6,2},{7,3},{8,12},{9,13},{10,... | collective-permute-start | bytes 20 | tf_op jit(solution)/shard_map/ppermute | solution.py:48
  331.1 4.6 %collective-permute-start.8 = (f32[]{:T(128)}, f32[]{:T(128)}, u32[]{:S(2)}, u32[]{:S(2)}) collective-permute-start(f32[]{:T(128)} %add.320), channel_id=1, source_target_pairs={{0,8},{1,9},{2,10},{3,11},{4,12},{5,13},{6,14},{7,15},{8,0},{9,1},... | collective-permute-start | bytes 20 | tf_op jit(solution)/shard_map/ppermute | solution.py:48
Sparse Core Ops, SparseCore 0:
  107.3 72.3 reduce-scatter.4
  183.7 133.9 reduce-scatter.2
